TPU v7x, 512 devices: a whole 4x8x8 slice. The times are simulated.
512 devices in a mesh: box: 128 (over x, y, z_hi), slab: 4 (over z_lo, core).
Axes of the slice: x: 4, y: 8, z: 8 (z_hi: 4, z_lo: 2; z = z_hi * 2 + z_lo), core: 2. Of those that a mesh axis runs over, the one named last changes fastest.
Arguments:
- velocity: bfloat16 [128, 3, 8, 16, 64, 128], P('box', None, None, None, 'slab'), may hold values from -6 to 6
- field: float32 [128, 3, 8, 16, 64], P('box', None, None, None, 'slab'), may hold values from -6 to 6
- conductivity: float32 [128, 8, 16, 64], P('box', None, None, 'slab'), may hold values from 0.5 to 2
- wall_flags: int32 [128, 8, 16, 64], P('box', None, None, 'slab'), may hold values 0 or 1
- leaf_solution: bfloat16 [128, 4, 512, 2048], P('box', 'slab'), may hold values from -0.125 to 0.125
- leaf_dtn: float32 [128, 4, 512, 512], P('box', 'slab'), as said below
Outputs:
- interface_two: float32 [128, 4, 256, 128], P('box', 'slab')
- neumann_two: float32 [128, 4, 512, 128], P('box', 'slab')
Inputs may be any that keep to these rules, and one draw needn't show every extreme that they name: `leaf_dtn`: every leaf map is symmetric positive definite.
All inputs are finite; a program needn't handle non-finite values. No bound on the sum of `wall_flags` on one device may be relied on, other than what follows from the above.
Results may differ from a plain program's by a relative error of at most 0.0029.
Values sent between devices are 32-bit elements; how exact they have to be, the bound alone decides.
No kernel may reach another device: no remote copies, remote signals or barrier semaphores. Data moves between devices by JAX's collectives and lax.ppermute only.
A program may use at most 64 MiB of HBM per device.

v0:
```python
import jax
import jax.numpy as jnp
from jax import lax
from jax.sharding import PartitionSpec as P

WALL_RATIO = 8.0
HIGHEST = lax.Precision.HIGHEST


def from_partner(block, axis, stride):
    count = lax.axis_size(axis)
    route = []
    for low in range(count):
        high = low | 1 << stride
        if high != low and high < count:
            route += [(low, high), (high, low)]
    return lax.ppermute(block, axis, route)


def padded_2(block, sides, width):
    for axis, dim in sides:
        count = lax.axis_size(axis)
        forward = [(i, i + 1) for i in range(count - 1)]
        backward = [(target, source) for source, target in forward]
        low = lax.ppermute(
            lax.slice_in_dim(block, block.shape[dim] - width, None, axis=dim), axis, forward
        )
        high = lax.ppermute(lax.slice_in_dim(block, 0, width, axis=dim), axis, backward)
        block = jnp.concatenate([low, block, high], axis=dim)
    return block


def currents(velocity, field, conductivity, wall_flags):
    sigma = conductivity * jnp.where(wall_flags == 1, WALL_RATIO, 1.0).astype(conductivity.dtype)
    speed = velocity.astype(jnp.float32)
    magnet = field[..., None]
    weight = sigma[..., None]
    elec_x = speed[1] * magnet[2] - speed[2] * magnet[1]
    elec_y = speed[2] * magnet[0] - speed[0] * magnet[2]
    elec_z = speed[0] * magnet[1] - speed[1] * magnet[0]
    return (weight * elec_x, weight * elec_y, weight * elec_z)


def divergence(flow_x, flow_y, padded_z):
    padded_x = jnp.pad(flow_x, ((1, 1), (0, 0), (0, 0), (0, 0)))
    padded_y = jnp.pad(flow_y, ((0, 0), (1, 1), (0, 0), (0, 0)))
    return 0.5 * (
        padded_x[2:]
        - padded_x[:-2]
        + (padded_y[:, 2:] - padded_y[:, :-2])
        + (padded_z[:, :, 2:] - padded_z[:, :, :-2])
    )


def schur_solve(schur, stacked):
    factor = jnp.linalg.cholesky(schur)
    return jax.scipy.linalg.cho_solve((factor, True), stacked)


def merge(left_map, left_data, right_map, right_data, need_map):
    width = left_map.shape[0] // 2
    schur = left_map[width:, width:] + right_map[:width, :width]
    coupling = jnp.concatenate([left_map[width:, :width], right_map[:width, width:]], axis=1)
    stacked = jnp.concatenate([coupling, left_data[width:] + right_data[:width]], axis=1)
    solved = schur_solve(schur, stacked)
    interface = -solved[:, 2 * width :]
    outward = jnp.concatenate([left_map[:width, width:], right_map[width:, :width]], axis=0)
    parent_data = jnp.concatenate([left_data[:width], right_data[width:]], axis=0) + jnp.dot(
        outward, interface, precision=HIGHEST
    )
    parent_map = None
    if need_map:
        zeros = jnp.zeros((width, width), left_map.dtype)
        base = jnp.concatenate(
            [
                jnp.concatenate([left_map[:width, :width], zeros], axis=1),
                jnp.concatenate([zeros, right_map[width:, width:]], axis=1),
            ],
            axis=0,
        )
        parent_map = base - jnp.dot(outward, solved[:, : 2 * width], precision=HIGHEST)
    return (parent_map, parent_data, interface)


def on_right_side(bit):
    return lax.axis_index("box") >> bit & 1 == 1


def merge_whole(dtn_map, neumann, bit, need_map):
    other_map, other_data = from_partner((dtn_map, neumann), "box", bit)
    right_side = on_right_side(bit)
    left_map = jnp.where(right_side, other_map, dtn_map)
    right_map = jnp.where(right_side, dtn_map, other_map)
    left_data = jnp.where(right_side, other_data, neumann)
    right_data = jnp.where(right_side, neumann, other_data)
    return merge(left_map, left_data, right_map, right_data, need_map)


def on_device(velocity, field, conductivity, wall_flags, leaf_solution, leaf_dtn):
    flow_x, flow_y, flow_z = currents(velocity[0], field[0], conductivity[0], wall_flags[0])
    solution_map = leaf_solution[0, 0]
    sizex, sizey, depth, snaps = flow_x.shape
    cell_count = sizex * sizey * depth
    padded = padded_2(flow_z, (("slab", 2),), 1)
    source = divergence(flow_x, flow_y, padded).astype(jnp.bfloat16)
    neumann = jnp.dot(
        solution_map, source.reshape(cell_count, snaps), preferred_element_type=jnp.float32
    )
    dtn_map = leaf_dtn[0, 0]
    map_one, neumann_one, first_face = merge_whole(dtn_map, neumann, 0, True)
    unused, neumann_two, interface_two = merge_whole(map_one, neumann_one, 1, False)
    return (interface_two[None, None], neumann_two[None, None])


def solution(mesh):
    return jax.shard_map(
        on_device,
        mesh=mesh,
        in_specs=(
            P("box", None, None, None, "slab", None),
            P("box", None, None, None, "slab"),
            P("box", None, None, "slab"),
            P("box", None, None, "slab"),
            P("box", "slab", None, None),
            P("box", "slab", None, None),
        ),
        out_specs=(P("box", "slab", None, None), P("box", "slab", None, None)),
        check_vma=False,
    )
```

profile of v0, /device:TPU:1, one launch (start us, length us, event | category | flops | bytes accessed | tf_op | source)
XLA Modules:
  0.0 288.1 jit_solution(3873890303489582429)
XLA Ops:
  0.7 1.9 convert_element_type.11
  2.7 2.2 subtract_multiply_fusion
  5.0 5.4 %collective-permute-start.2 = (f32[8,16,1,128]{3,2,1,0:T(1,128)S(1)}, f32[8,16,1,128]{3,2,1,0:T(1,128)S(1)}, u32[]{:S(2)}, u32[]{:S(2)}) collective-permute-start(f32[8,16,1,128]{3,2,1,0:T(1,128)S(1)} %get-tuple-element.62), channel_id=1, source_target_pairs={{0,1},{1,2},{2,3},{4,5},{5,6},{6,7},{8,9},{9,10},{10,11},{12,13},{... | collective-permute-start | bytes 196616 | tf_op jit(solution)/shard_map/ppermute | solution.py:25
  10.4 4.7 %collective-permute-start.1 = (f32[8,16,1,128]{3,2,1,0:T(1,128)S(1)}, f32[8,16,1,128]{3,2,1,0:T(1,128)S(1)}, u32[]{:S(2)}, u32[]{:S(2)}) collective-permute-start(f32[8,16,1,128]{3,2,1,0:T(1,128)S(1)} %get-tuple-element.61), channel_id=1, source_target_pairs={{1,0},{2,1},{3,2},{5,4},{6,5},{7,6},{9,8},{10,9},{11,10},{13,12},{... | collective-permute-start | bytes 196616 | tf_op jit(solution)/shard_map/ppermute | solution.py:28
  15.0 2.6 copy.8
  17.6 3.1 %collective-permute-start = (f32[512,512]{0,1:T(8,128)}, f32[512,512]{0,1:T(8,128)}, u32[]{:S(2)}, u32[]{:S(2)}) collective-permute-start(f32[512,512]{0,1:T(8,128)} %bitcast.114), channel_id=1, source_target_pairs={{0,4},{4,0},{8,12},{12,8},{16,20},{20,16},{24,28},{28,24},{32,36},... | collective-permute-start | bytes 3145736 | tf_op jit(solution)/shard_map/ppermute | solution.py:17
  20.7 2.6 fusion.9
  24.1 3.4 %collective-permute-start.3 = (f32[512,128]{0,1:T(8,128)S(1)}, f32[512,128]{0,1:T(8,128)}, u32[]{:S(2)}, u32[]{:S(2)}) collective-permute-start(f32[512,128]{0,1:T(8,128)S(1)} %fusion.2), channel_id=1, source_target_pairs={{0,4},{4,0},{8,12},{12,8},{16,20},{20,16},{24,28},{28,24},{32,36},... | collective-permute-start | bytes 786440 | tf_op jit(solution)/shard_map/ppermute | solution.py:17
  27.5 50.7 %collective-permute-done.3 = f32[512,128]{0,1:T(8,128)} collective-permute-done((f32[512,128]{0,1:T(8,128)S(1)}, f32[512,128]{0,1:T(8,128)}, u32[]{:S(2)}, u32[]{:S(2)}) %collective-permute-start.3) | collective-permute-done | bytes 262176 | tf_op jit(solution)/shard_map/ppermute | solution.py:17
  79.9 1.4 broadcast_select_fusion.1
  83.2 11.7 %cholesky.130 = f32[128,128]{1,0:T(8,128)S(1)} custom-call(f32[128,128]{1,0:T(8,128)S(1)} %cholesky.194), custom_call_target="Cholesky" | custom-call | tf_op jit(solution)/shard_map/jit(cholesky)/cholesky | solution.py:56
  95.0 9.8 %custom-call.15 = f32[1,128,128]{1,2,0:T(8,128)S(1)} custom-call(f32[1,128,128]{2,1,0:T(8,128)S(1)} %get-tuple-element.83), custom_call_target="InvertDiagBlocksLowerTriangular" | custom-call | tf_op jit(solution)/shard_map/jit(cholesky)/cholesky | solution.py:56
  107.0 11.7 %cholesky.147 = f32[128,128]{1,0:T(8,128)S(1)} custom-call(f32[128,128]{1,0:T(8,128)S(1)} %convolution_subtract_fusion.5), custom_call_target="Cholesky" | custom-call | tf_op jit(solution)/shard_map/jit(cholesky)/cholesky | solution.py:56
  120.9 4.7 %while.4 = (s32[]{:T(128)}, f32[256,256]{1,0:T(8,128)S(1)}, s32[2,2]{1,0:T(2,128)S(1)}, f32[2,128,128]{2,1,0:T(8,128)S(1)}, s32[]{:T(128)}) while((s32[]{:T(128)}, f32[256,256]{1,0:T(8,128)S(1)}, s32[2,2]{1,0:T(2,128)S(1)}, f32[2,128,128]{2,1,0:T(8,128)S(1)}, s32[]{:T(128)}) %tuple.71), condition=%wide.while_cond, body=%wide.while_body.sunk | while | flops 2 | bytes 131189 | solution.py:57
  122.1 1.4 bitcast_dynamic-update-slice_fusion.4
  124.2 1.4 bitcast_dynamic-update-slice_fusion.4
  125.6 19.7 %custom-call.16 = f32[2,128,128]{1,2,0:T(8,128)S(1)} custom-call(f32[2,128,128]{2,1,0:T(8,128)S(1)} %get-tuple-element.18), custom_call_target="InvertDiagBlocksLowerTriangular" | custom-call | tf_op jit(solution)/shard_map/jit(_cho_solve)/triangular_solve | solution.py:57
  149.5 6.7 %collective-permute-start.4 = (f32[512,512]{0,1:T(8,128)S(1)}, f32[512,512]{0,1:T(8,128)}, u32[]{:S(2)}, u32[]{:S(2)}) collective-permute-start(f32[512,512]{0,1:T(8,128)S(1)} %fusion.12), channel_id=1, source_target_pairs={{0,8},{8,0},{4,12},{12,4},{16,24},{24,16},{20,28},{28,20},{32,40},... | collective-permute-start | bytes 3145736 | tf_op jit(solution)/shard_map/ppermute | solution.py:17
  156.2 1.4 maximum_add_fusion
  157.6 2.7 collective-permute-start.5
  160.3 53.4 %collective-permute-done.5 = f32[512,128]{0,1:T(8,128)} collective-permute-done((f32[512,128]{0,1:T(8,128)S(1)}, f32[512,128]{0,1:T(8,128)}, u32[]{:S(2)}, u32[]{:S(2)}) %collective-permute-start.5) | collective-permute-done | bytes 262176 | tf_op jit(solution)/shard_map/ppermute | solution.py:17
  215.5 1.4 broadcast_select_fusion.3
  218.6 11.7 %cholesky.164 = f32[128,128]{1,0:T(8,128)S(1)} custom-call(f32[128,128]{1,0:T(8,128)S(1)} %cholesky.197), custom_call_target="Cholesky" | custom-call | tf_op jit(solution)/shard_map/jit(cholesky)/cholesky | solution.py:56
  230.4 9.8 %custom-call.17 = f32[1,128,128]{1,2,0:T(8,128)S(1)} custom-call(f32[1,128,128]{2,1,0:T(8,128)S(1)} %get-tuple-element.79), custom_call_target="InvertDiagBlocksLowerTriangular" | custom-call | tf_op jit(solution)/shard_map/jit(cholesky)/cholesky | solution.py:56
  241.3 1.1 convolution_subtract_fusion.4
  242.4 11.7 %cholesky.181 = f32[128,128]{1,0:T(8,128)S(1)} custom-call(f32[128,128]{1,0:T(8,128)S(1)} %convolution_subtract_fusion.4), custom_call_target="Cholesky" | custom-call | tf_op jit(solution)/shard_map/jit(cholesky)/cholesky | solution.py:56
  256.8 4.2 %while.5 = (s32[]{:T(128)}, f32[256,256]{1,0:T(8,128)S(1)}, s32[2,2]{1,0:T(2,128)S(1)}, f32[2,128,128]{2,1,0:T(8,128)S(1)}, s32[]{:T(128)}) while((s32[]{:T(128)}, f32[256,256]{1,0:T(8,128)S(1)}, s32[2,2]{1,0:T(2,128)S(1)}, f32[2,128,128]{2,1,0:T(8,128)S(1)}, s32[]{:T(128)}) %tuple.77), condition=%wide.while_cond.clone, body=%wide.while_body.clone.sunk | while | flops 2 | bytes 131189 | solution.py:57
  257.7 1.3 bitcast_dynamic-update-slice_fusion.5
  259.7 1.3 bitcast_dynamic-update-slice_fusion.5
  261.0 19.7 %custom-call.18 = f32[2,128,128]{1,2,0:T(8,128)S(1)} custom-call(f32[2,128,128]{2,1,0:T(8,128)S(1)} %get-tuple-element.19), custom_call_target="InvertDiagBlocksLowerTriangular" | custom-call | tf_op jit(solution)/shard_map/jit(_cho_solve)/triangular_solve | solution.py:57
  283.0 1.4 fusion.51
  284.4 1.3 fusion.50
  (98 shorter events, 24.6 us)
Async XLA Ops:
  0.6 22.6 %copy-start = (bf16[1,1,512,2048]{3,2,1,0:T(8,128)(2,1)S(1)}, bf16[1,1,512,2048]{3,2,1,0:T(8,128)(2,1)}, u32[]{:S(2)}) copy-start(bf16[1,1,512,2048]{3,2,1,0:T(8,128)(2,1)} %param.13) | copy-start | bytes 6291460
  0.6 1.9 copy-start.15
  0.7 2.0 copy-start.16
  0.7 2.0 copy-start.17
  5.0 15.7 %collective-permute-start.2 = (f32[8,16,1,128]{3,2,1,0:T(1,128)S(1)}, f32[8,16,1,128]{3,2,1,0:T(1,128)S(1)}, u32[]{:S(2)}, u32[]{:S(2)}) collective-permute-start(f32[8,16,1,128]{3,2,1,0:T(1,128)S(1)} %get-tuple-element.62), channel_id=1, source_target_pairs={{0,1},{1,2},{2,3},{4,5},{5,6},{6,7},{8,9},{9,10},{10,11},{12,13},{... | collective-permute-start | bytes 196616 | tf_op jit(solution)/shard_map/ppermute | solution.py:25
  10.4 10.3 %collective-permute-start.1 = (f32[8,16,1,128]{3,2,1,0:T(1,128)S(1)}, f32[8,16,1,128]{3,2,1,0:T(1,128)S(1)}, u32[]{:S(2)}, u32[]{:S(2)}) collective-permute-start(f32[8,16,1,128]{3,2,1,0:T(1,128)S(1)} %get-tuple-element.61), channel_id=1, source_target_pairs={{1,0},{2,1},{3,2},{5,4},{6,5},{7,6},{9,8},{10,9},{11,10},{13,12},{... | collective-permute-start | bytes 196616 | tf_op jit(solution)/shard_map/ppermute | solution.py:28
  17.6 62.3 %collective-permute-start = (f32[512,512]{0,1:T(8,128)}, f32[512,512]{0,1:T(8,128)}, u32[]{:S(2)}, u32[]{:S(2)}) collective-permute-start(f32[512,512]{0,1:T(8,128)} %bitcast.114), channel_id=1, source_target_pairs={{0,4},{4,0},{8,12},{12,8},{16,20},{20,16},{24,28},{28,24},{32,36},... | collective-permute-start | bytes 3145736 | tf_op jit(solution)/shard_map/ppermute | solution.py:17
  23.2 56.7 %copy-start.1 = (f32[1,1,512,512]{2,3,1,0:T(8,128)S(1)}, f32[1,1,512,512]{2,3,1,0:T(8,128)}, u32[]{:S(2)}) copy-start(f32[1,1,512,512]{2,3,1,0:T(8,128)} %copy.8) | copy-start | bytes 3145732
  24.1 54.1 %collective-permute-start.3 = (f32[512,128]{0,1:T(8,128)S(1)}, f32[512,128]{0,1:T(8,128)}, u32[]{:S(2)}, u32[]{:S(2)}) collective-permute-start(f32[512,128]{0,1:T(8,128)S(1)} %fusion.2), channel_id=1, source_target_pairs={{0,4},{4,0},{8,12},{12,8},{16,20},{20,16},{24,28},{28,24},{32,36},... | collective-permute-start | bytes 786440 | tf_op jit(solution)/shard_map/ppermute | solution.py:17
  82.3 66.1 %copy-start.3 = (f32[256,256]{0,1:T(8,128)}, f32[256,256]{0,1:T(8,128)S(1)}, u32[]{:S(2)}) copy-start(f32[256,256]{0,1:T(8,128)S(1)} %get-tuple-element.58) | copy-start | bytes 786436
  82.5 0.7 copy-start.5
  145.8 2.6 copy-start.4
  145.8 2.6 copy-start.13
  145.8 2.6 copy-start.14
  148.0 8.2 %copy-start.9 = (f32[256,128]{0,1:T(8,128)S(1)}, f32[256,128]{0,1:T(8,128)}, u32[]{:S(2)}) copy-start(f32[256,128]{0,1:T(8,128)} %get-tuple-element.71) | copy-start | bytes 393220
  148.0 8.2 %copy-start.10 = (f32[256,128]{0,1:T(8,128)S(1)}, f32[256,128]{0,1:T(8,128)}, u32[]{:S(2)}) copy-start(f32[256,128]{0,1:T(8,128)} %get-tuple-element.72) | copy-start | bytes 393220
  149.5 66.0 %collective-permute-start.4 = (f32[512,512]{0,1:T(8,128)S(1)}, f32[512,512]{0,1:T(8,128)}, u32[]{:S(2)}, u32[]{:S(2)}) collective-permute-start(f32[512,512]{0,1:T(8,128)S(1)} %fusion.12), channel_id=1, source_target_pairs={{0,8},{8,0},{4,12},{12,4},{16,24},{24,16},{20,28},{28,20},{32,40},... | collective-permute-start | bytes 3145736 | tf_op jit(solution)/shard_map/ppermute | solution.py:17
  157.6 56.1 %collective-permute-start.5 = (f32[512,128]{0,1:T(8,128)S(1)}, f32[512,128]{0,1:T(8,128)}, u32[]{:S(2)}, u32[]{:S(2)}) collective-permute-start(f32[512,128]{0,1:T(8,128)S(1)} %maximum_add_fusion), channel_id=1, source_target_pairs={{0,8},{8,0},{4,12},{12,4},{16,24},{24,16},{20,28},{28,20},{32,40},... | collective-permute-start | bytes 786440 | tf_op jit(solution)/shard_map/ppermute | solution.py:17
  217.9 0.7 copy-start.6
  280.7 1.5 copy-start.11
  282.9 3.2 %copy-start.12 = (f32[2,128,128]{1,2,0:T(8,128)S(1)}, f32[2,128,128]{1,2,0:T(8,128)}, u32[]{:S(2)}) copy-start(f32[2,128,128]{1,2,0:T(8,128)} %copy-done.11) | copy-start | bytes 393220
  282.9 3.6 %copy-start.2 = (f32[256,256]{0,1:T(8,128)S(1)}, f32[256,256]{0,1:T(8,128)}, u32[]{:S(2)}) copy-start(f32[256,256]{0,1:T(8,128)} %get-tuple-element.52) | copy-start | bytes 786436
  283.0 3.6 %copy-start.7 = (f32[256,128]{0,1:T(8,128)S(1)}, f32[256,128]{0,1:T(8,128)}, u32[]{:S(2)}) copy-start(f32[256,128]{0,1:T(8,128)} %get-tuple-element.69) | copy-start | bytes 393220
  286.6 1.4 copy-start.8
where the time goes:
time: 292 us; the launch traced here: 288 us
  other arithmetic  124 us (42%)
  waiting for transfers between devices  104 us (36%)
  starting transfers between devices  25.9 us (9%)
  matrix products  15.8 us (5%)
  local copies, waits for them, and re-layouts  13.4 us (5%)
  between operations  4.09 us (1%)
    ppermute x4, waiting for transfers between devices, from_partner(): return lax.ppermute(block, axis, route)  104 us
    another operation x13, other arithmetic, schur_solve(): factor = jnp.linalg.cholesky(schur)  68.7 us
    another operation x5, other arithmetic, schur_solve(): return jax.scipy.linalg.cho_solve((factor, True), stacked)  39.4 us
    ppermute x4, starting transfers between devices, from_partner(): return lax.ppermute(block, axis, route)  15.8 us
    another operation x15, local copies, waits for them, and re-layouts, schur_solve(): return jax.scipy.linalg.cho_solve((factor, True), stacked)  8.15 us
    another operation x12, matrix products, schur_solve(): return jax.scipy.linalg.cho_solve((factor, True), stacked)  7.73 us
  transfers between devices with their start and end apart: 6, of which 2 were waited for; matrix products, arithmetic and copies ran while one was open for 4% of the time, Pallas kernels for 0%

commit v1 on v0

v1 whole, which is shorter than its diff:
```python
import jax
import jax.numpy as jnp
from jax import lax
from jax.sharding import PartitionSpec as P

WALL_RATIO = 8.0
HIGHEST = lax.Precision.HIGHEST


def padded_2(block, sides, width):
    for axis, dim in sides:
        count = lax.axis_size(axis)
        forward = [(i, i + 1) for i in range(count - 1)]
        backward = [(target, source) for source, target in forward]
        low = lax.ppermute(
            lax.slice_in_dim(block, block.shape[dim] - width, None, axis=dim), axis, forward
        )
        high = lax.ppermute(lax.slice_in_dim(block, 0, width, axis=dim), axis, backward)
        block = jnp.concatenate([low, block, high], axis=dim)
    return block


def currents(velocity, field, conductivity, wall_flags):
    sigma = conductivity * jnp.where(wall_flags == 1, WALL_RATIO, 1.0).astype(conductivity.dtype)
    speed = velocity.astype(jnp.float32)
    magnet = field[..., None]
    weight = sigma[..., None]
    elec_x = speed[1] * magnet[2] - speed[2] * magnet[1]
    elec_y = speed[2] * magnet[0] - speed[0] * magnet[2]
    elec_z = speed[0] * magnet[1] - speed[1] * magnet[0]
    return (weight * elec_x, weight * elec_y, weight * elec_z)


def divergence(flow_x, flow_y, padded_z):
    padded_x = jnp.pad(flow_x, ((1, 1), (0, 0), (0, 0), (0, 0)))
    padded_y = jnp.pad(flow_y, ((0, 0), (1, 1), (0, 0), (0, 0)))
    return 0.5 * (
        padded_x[2:]
        - padded_x[:-2]
        + (padded_y[:, 2:] - padded_y[:, :-2])
        + (padded_z[:, :, 2:] - padded_z[:, :, :-2])
    )


def schur_solve(schur, stacked):
    factor = jnp.linalg.cholesky(schur)
    return jax.scipy.linalg.cho_solve((factor, True), stacked)


def dot(a, b):
    return jnp.dot(a, b, precision=HIGHEST)


def group_route(count, pairs):
    route = []
    for base in range(0, count, 4):
        route += [(base + s, base + t) for s, t in pairs]
    return route


def take(block, start, size, axis):
    return lax.dynamic_slice_in_dim(block, start, size, axis=axis)


def on_device(velocity, field, conductivity, wall_flags, leaf_solution, leaf_dtn):
    count = lax.axis_size("box")
    dtn_map = leaf_dtn[0, 0]
    width = dtn_map.shape[0] // 2
    place = lax.axis_index("box") % 4
    odd = place % 2
    near = (1 - odd) * width
    far = odd * width

    inward = group_route(count, [(0, 1), (3, 2)])
    sent_map = lax.ppermute(take(dtn_map, near, width, 1), "box", inward)

    flow_x, flow_y, flow_z = currents(velocity[0], field[0], conductivity[0], wall_flags[0])
    solution_map = leaf_solution[0, 0]
    sizex, sizey, depth, snaps = flow_x.shape
    cell_count = sizex * sizey * depth
    padded = padded_2(flow_z, (("slab", 2),), 1)
    source = divergence(flow_x, flow_y, padded).astype(jnp.bfloat16)
    neumann = jnp.dot(
        solution_map, source.reshape(cell_count, snaps), preferred_element_type=jnp.float32
    )
    sent_data = lax.ppermute(neumann, "box", inward)

    own_nn = take(take(dtn_map, near, width, 0), near, width, 1)
    own_nf = take(take(dtn_map, near, width, 0), far, width, 1)
    own_fn = take(take(dtn_map, far, width, 0), near, width, 1)
    own_ff = take(take(dtn_map, far, width, 0), far, width, 1)
    part_nn = take(sent_map, far, width, 0)
    part_fn = take(sent_map, near, width, 0)
    schur = own_nn + part_nn
    rhs = take(neumann, near, width, 0) + take(sent_data, far, width, 0)
    solved = schur_solve(schur, jnp.concatenate([own_nf, rhs], axis=1))
    solved_map = solved[:, :width]
    first_face = -solved[:, width:]
    far_map = own_ff - dot(own_fn, solved_map)
    cross_map = -dot(part_fn, solved_map)
    far_data = take(neumann, far, width, 0) + dot(own_fn, first_face)
    part_data = take(sent_data, near, width, 0) + dot(part_fn, first_face)

    swap = group_route(count, [(1, 2), (2, 1)])
    other = lax.ppermute(jnp.concatenate([far_map, far_data], axis=1), "box", swap)
    schur_two = far_map + other[:, :width]
    rhs_two = far_data + other[:, width:]
    interface_two = -schur_solve(schur_two, rhs_two)
    half = part_data + dot(cross_map, interface_two)

    outer = lax.ppermute(
        jnp.concatenate([interface_two, half], axis=1), "box", group_route(count, [(1, 0), (2, 3)])
    )
    inner = lax.ppermute(half, "box", swap)
    across = lax.ppermute(half, "box", group_route(count, [(1, 3), (2, 0)]))
    snaps_two = interface_two.shape[1]
    is_inner = (place == 1) | (place == 2)
    interface_out = jnp.where(is_inner, interface_two, outer[:, :snaps_two])
    outer_half = outer[:, snaps_two:]
    top = jnp.where(
        place == 0, outer_half, jnp.where(place == 1, half, jnp.where(place == 2, inner, across))
    )
    bottom = jnp.where(
        place == 0, across, jnp.where(place == 1, inner, jnp.where(place == 2, half, outer_half))
    )
    neumann_two = jnp.concatenate([top, bottom], axis=0)
    return (interface_out[None, None], neumann_two[None, None])


def solution(mesh):
    return jax.shard_map(
        on_device,
        mesh=mesh,
        in_specs=(
            P("box", None, None, None, "slab", None),
            P("box", None, None, None, "slab"),
            P("box", None, None, "slab"),
            P("box", None, None, "slab"),
            P("box", "slab", None, None),
            P("box", "slab", None, None),
        ),
        out_specs=(P("box", "slab", None, None), P("box", "slab", None, None)),
        check_vma=False,
    )
```

time: 292 us -> 262 us (0.90)
  waiting for transfers between devices: 104 us -> 58.6 us
  local copies, waits for them, and re-layouts: 13.4 us -> 27 us
  starting transfers between devices: 25.9 us -> 19.8 us
  other arithmetic: 124 us -> 130 us
  matrix products: 15.8 us -> 20.5 us
    ppermute x4 -> x6, waiting for transfers between devices: 104 us -> 58.6 us  [the longest x1 53.7 us: on_device(): across = lax.ppermute(half, 'box', group_route(count, [(1, 3), (2, 0)]))]
    another operation x0 -> x12, local copies, waits for them, and re-layouts: none -> 10.7 us
    another operation x15 -> x2, local copies, waits for them, and re-layouts: 8.15 us -> 0.16 us  [schur_solve(): return jax.scipy.linalg.cho_solve((factor, True), stacked)]
    dynamic_slice x0 -> x5, local copies, waits for them, and re-layouts: none -> 7.59 us  [take(): return lax.dynamic_slice_in_dim(block, start, size, axis=axis)]
    another operation x13, other arithmetic: 68.7 us -> 75.8 us  [schur_solve(): factor = jnp.linalg.cholesky(schur)]
    ppermute x4 -> x6, starting transfers between devices: 15.8 us -> 9.79 us  [the longest x1 3.86 us: on_device(): sent_map = lax.ppermute(take(dtn_map, near, width, 1), 'box', inward)]
    select_n x4 -> x1, other arithmetic: 4.88 us -> 0.05 us  [on_device(): jnp.where(place == 0, outer_half, jnp.where(place == 1, half, jnp.where(p...]
    add x1 -> x4, other arithmetic: 0.73 us -> 3.96 us  [the longest x1 1.07 us: on_device(): schur = own_nn + part_nn]
  transfers between devices with their start and end apart: 6 -> 8, of which waited for: 2 -> 2; matrix products, arithmetic and copies ran while one was open for 4% -> 5% of each run, Pallas kernels for 0% -> 0%
where the time goes in v1:
time: 262 us; the launch traced here: 260 us
  other arithmetic  130 us (50%)
  waiting for transfers between devices  58.6 us (22%)
  local copies, waits for them, and re-layouts  27 us (10%)
  matrix products  20.5 us (8%)
  starting transfers between devices  19.8 us (8%)
  between operations  3.69 us (1%)
    another operation x13, other arithmetic, schur_solve(): factor = jnp.linalg.cholesky(schur)  75.8 us
    ppermute x1, waiting for transfers between devices, on_device(): across = lax.ppermute(half, 'box', group_route(count, [(1, 3), (2, 0)]))  53.7 us
    another operation x5, other arithmetic, schur_solve(): return jax.scipy.linalg.cho_solve((factor, True), stacked)  42.5 us
    another operation x12, local copies, waits for them, and re-layouts  10.7 us
    another operation x12, matrix products, schur_solve(): return jax.scipy.linalg.cho_solve((factor, True), stacked)  7.94 us
    dynamic_slice x5, local copies, waits for them, and re-layouts, take(): return lax.dynamic_slice_in_dim(block, start, size, axis=axis)  7.59 us
    another operation x4, matrix products, schur_solve(): factor = jnp.linalg.cholesky(schur)  5.59 us
    dot_general x5, matrix products, dot(): return jnp.dot(a, b, precision=HIGHEST)  5.43 us
  transfers between devices with their start and end apart: 8, of which 2 were waited for; matrix products, arithmetic and copies ran while one was open for 5% of the time, Pallas kernels for 0%

profile of v1, /device:TPU:1, one launch (start us, length us, event | category | flops | bytes accessed | tf_op | source)
XLA Modules:
  0.0 260.1 jit_solution(13302618740424750845)
XLA Ops:
  0.7 1.9 convert_element_type.11
  2.7 2.2 subtract_multiply_fusion
  5.0 5.4 %collective-permute-start.2 = (f32[8,16,1,128]{3,2,1,0:T(1,128)S(1)}, f32[8,16,1,128]{3,2,1,0:T(1,128)S(1)}, u32[]{:S(2)}, u32[]{:S(2)}) collective-permute-start(f32[8,16,1,128]{3,2,1,0:T(1,128)S(1)} %get-tuple-element.48), channel_id=1, source_target_pairs={{0,1},{1,2},{2,3},{4,5},{5,6},{6,7},{8,9},{9,10},{10,11},{12,13},{... | collective-permute-start | bytes 196616 | tf_op jit(solution)/shard_map/ppermute | solution.py:15
  10.4 4.7 %collective-permute-start.1 = (f32[8,16,1,128]{3,2,1,0:T(1,128)S(1)}, f32[8,16,1,128]{3,2,1,0:T(1,128)S(1)}, u32[]{:S(2)}, u32[]{:S(2)}) collective-permute-start(f32[8,16,1,128]{3,2,1,0:T(1,128)S(1)} %get-tuple-element.47), channel_id=1, source_target_pairs={{1,0},{2,1},{3,2},{5,4},{6,5},{7,6},{9,8},{10,9},{11,10},{13,12},{... | collective-permute-start | bytes 196616 | tf_op jit(solution)/shard_map/ppermute | solution.py:18
  15.1 1.9 constant_dynamic-slice_fusion.2
  17.0 2.0 copy.10
  19.0 3.9 %collective-permute-start = (f32[512,256]{0,1:T(8,128)}, f32[512,256]{0,1:T(8,128)}, u32[]{:S(2)}, u32[]{:S(2)}) collective-permute-start(f32[512,256]{0,1:T(8,128)} %bitcast.124), channel_id=1, source_target_pairs={{0,4},{12,8},{16,20},{28,24},{32,36},{44,40},{48,52},{60,56},{64,6... | collective-permute-start | bytes 1572872 | tf_op jit(solution)/shard_map/ppermute | solution.py:75
  22.9 2.5 fusion.6
  25.4 1.5 fusion
  27.0 2.0 collective-permute-start.3
  30.0 1.8 copy.9
  32.6 4.9 %collective-permute-done.3 = f32[512,128]{0,1:T(8,128)} collective-permute-done((f32[512,128]{0,1:T(8,128)}, f32[512,128]{0,1:T(8,128)}, u32[]{:S(2)}, u32[]{:S(2)}) %collective-permute-start.3) | collective-permute-done | bytes 262176 | tf_op jit(solution)/shard_map/ppermute | solution.py:86
  42.9 13.2 %cholesky.130 = f32[128,128]{1,0:T(8,128)} custom-call(f32[128,128]{1,0:T(8,128)} %cholesky.194), custom_call_target="Cholesky" | custom-call | tf_op jit(solution)/shard_map/jit(cholesky)/cholesky | solution.py:46
  56.1 1.5 fusion.39
  57.5 1.6 cholesky.155
  59.1 11.3 %custom-call.25 = f32[1,128,128]{1,2,0:T(8,128)} custom-call(f32[1,128,128]{2,1,0:T(8,128)} %get-tuple-element.62), custom_call_target="InvertDiagBlocksLowerTriangular" | custom-call | tf_op jit(solution)/shard_map/jit(cholesky)/cholesky | solution.py:46
  70.4 1.7 constant_dynamic-update-slice_fusion.1
  72.1 1.7 convolution_subtract_fusion.4
  73.8 13.2 %cholesky.147 = f32[128,128]{1,0:T(8,128)} custom-call(f32[128,128]{1,0:T(8,128)} %convolution_subtract_fusion.4), custom_call_target="Cholesky" | custom-call | tf_op jit(solution)/shard_map/jit(cholesky)/cholesky | solution.py:46
  87.0 1.5 fusion.40
  90.3 1.7 select_select_fusion.1
  92.7 6.8 %while.2 = (s32[]{:T(128)}, f32[256,256]{1,0:T(8,128)}, s32[2,2]{1,0:T(2,128)S(1)}, f32[2,128,128]{2,1,0:T(8,128)}, s32[]{:T(128)}) while((s32[]{:T(128)}, f32[256,256]{1,0:T(8,128)}, s32[2,2]{1,0:T(2,128)S(1)}, f32[2,128,128]{2,1,0:T(8,128)}, s32[]{:T(128)}) %tuple.55), condition=%wide.while_cond, body=%wide.while_body.sunk | while | flops 2 | bytes 132205 | solution.py:47
  93.3 2.9 %bitcast_dynamic-update-slice_fusion.4 = f32[2,128,128]{2,1,0:T(8,128)} fusion(f32[2,128,128]{2,1,0:T(8,128)} %get-tuple-element.135, s32[]{:T(128)S(6)} %copy.29, f32[256,256]{1,0:T(8,128)} %get-tuple-element.138, s32[]{:T(128)} %bitcast.118, s32[]{:T(128)} %bitcast.119), kind=kLoop, calls=%fused_computation.clone.1 | loop fusion | bytes 132100 | tf_op jit(solution)/shard_map/jit(_cho_solve)/triangular_solve
  96.8 2.8 %bitcast_dynamic-update-slice_fusion.4 = f32[2,128,128]{2,1,0:T(8,128)} fusion(f32[2,128,128]{2,1,0:T(8,128)} %get-tuple-element.135, s32[]{:T(128)S(6)} %copy.29, f32[256,256]{1,0:T(8,128)} %get-tuple-element.138, s32[]{:T(128)} %bitcast.118, s32[]{:T(128)} %bitcast.119), kind=kLoop, calls=%fused_computation.clone.1 | loop fusion | bytes 132100 | tf_op jit(solution)/shard_map/jit(_cho_solve)/triangular_solve
  99.6 21.1 %custom-call.22 = f32[2,128,128]{1,2,0:T(8,128)} custom-call(f32[2,128,128]{2,1,0:T(8,128)} %get-tuple-element.10), custom_call_target="InvertDiagBlocksLowerTriangular" | custom-call | tf_op jit(solution)/shard_map/jit(_cho_solve)/triangular_solve | solution.py:47
  130.6 1.6 convolution_negate_fusion
  134.8 11.7 %cholesky.164 = f32[128,128]{1,0:T(8,128)S(1)} custom-call(f32[128,128]{1,0:T(8,128)S(1)} %cholesky.197), custom_call_target="Cholesky" | custom-call | tf_op jit(solution)/shard_map/jit(cholesky)/cholesky | solution.py:46
  146.6 9.8 %custom-call.26 = f32[1,128,128]{1,2,0:T(8,128)S(1)} custom-call(f32[1,128,128]{2,1,0:T(8,128)S(1)} %get-tuple-element.58), custom_call_target="InvertDiagBlocksLowerTriangular" | custom-call | tf_op jit(solution)/shard_map/jit(cholesky)/cholesky | solution.py:46
  158.6 11.7 %cholesky.181 = f32[128,128]{1,0:T(8,128)S(1)} custom-call(f32[128,128]{1,0:T(8,128)S(1)} %convolution_subtract_fusion.3), custom_call_target="Cholesky" | custom-call | tf_op jit(solution)/shard_map/jit(cholesky)/cholesky | solution.py:46
  172.9 4.2 %while.3 = (s32[]{:T(128)}, f32[256,256]{1,0:T(8,128)S(1)}, s32[2,2]{1,0:T(2,128)S(1)}, f32[2,128,128]{2,1,0:T(8,128)S(1)}, s32[]{:T(128)}) while((s32[]{:T(128)}, f32[256,256]{1,0:T(8,128)S(1)}, s32[2,2]{1,0:T(2,128)S(1)}, f32[2,128,128]{2,1,0:T(8,128)S(1)}, s32[]{:T(128)}) %tuple.61), condition=%wide.while_cond.1, body=%wide.while_body.1.sunk | while | flops 2 | bytes 131189 | solution.py:47
  177.1 19.7 %custom-call.23 = f32[2,128,128]{1,2,0:T(8,128)S(1)} custom-call(f32[2,128,128]{2,1,0:T(8,128)S(1)} %get-tuple-element.18), custom_call_target="InvertDiagBlocksLowerTriangular" | custom-call | tf_op jit(solution)/shard_map/jit(_cho_solve)/triangular_solve | solution.py:47
  204.7 53.7 %collective-permute-done.7 = f32[256,128]{0,1:T(8,128)S(1)} collective-permute-done((f32[256,128]{0,1:T(8,128)S(1)}, f32[256,128]{0,1:T(8,128)S(1)}, u32[]{:S(2)}, u32[]{:S(2)}) %collective-permute-start.7) | collective-permute-done | bytes 131104 | tf_op jit(solution)/shard_map/ppermute | solution.py:115
  (101 shorter events, 39.1 us)
Async XLA Ops:
  0.6 24.8 %copy-start = (bf16[1,1,512,2048]{3,2,1,0:T(8,128)(2,1)S(1)}, bf16[1,1,512,2048]{3,2,1,0:T(8,128)(2,1)}, u32[]{:S(2)}) copy-start(bf16[1,1,512,2048]{3,2,1,0:T(8,128)(2,1)} %param.11) | copy-start | bytes 6291460
  0.6 1.9 copy-start.11
  0.7 2.0 copy-start.12
  0.7 2.0 copy-start.13
  5.0 17.9 %collective-permute-start.2 = (f32[8,16,1,128]{3,2,1,0:T(1,128)S(1)}, f32[8,16,1,128]{3,2,1,0:T(1,128)S(1)}, u32[]{:S(2)}, u32[]{:S(2)}) collective-permute-start(f32[8,16,1,128]{3,2,1,0:T(1,128)S(1)} %get-tuple-element.48), channel_id=1, source_target_pairs={{0,1},{1,2},{2,3},{4,5},{5,6},{6,7},{8,9},{9,10},{10,11},{12,13},{... | collective-permute-start | bytes 196616 | tf_op jit(solution)/shard_map/ppermute | solution.py:15
  10.4 12.5 %collective-permute-start.1 = (f32[8,16,1,128]{3,2,1,0:T(1,128)S(1)}, f32[8,16,1,128]{3,2,1,0:T(1,128)S(1)}, u32[]{:S(2)}, u32[]{:S(2)}) collective-permute-start(f32[8,16,1,128]{3,2,1,0:T(1,128)S(1)} %get-tuple-element.47), channel_id=1, source_target_pairs={{1,0},{2,1},{3,2},{5,4},{6,5},{7,6},{9,8},{10,9},{11,10},{13,12},{... | collective-permute-start | bytes 196616 | tf_op jit(solution)/shard_map/ppermute | solution.py:18
  19.0 19.6 %collective-permute-start = (f32[512,256]{0,1:T(8,128)}, f32[512,256]{0,1:T(8,128)}, u32[]{:S(2)}, u32[]{:S(2)}) collective-permute-start(f32[512,256]{0,1:T(8,128)} %bitcast.124), channel_id=1, source_target_pairs={{0,4},{12,8},{16,20},{28,24},{32,36},{44,40},{48,52},{60,56},{64,6... | collective-permute-start | bytes 1572872 | tf_op jit(solution)/shard_map/ppermute | solution.py:75
  25.4 3.6 %copy-start.1 = (f32[1,1,512,512]{3,2,1,0:T(8,128)S(1)}, f32[1,1,512,512]{3,2,1,0:T(8,128)}, u32[]{:S(2)}) copy-start(f32[1,1,512,512]{3,2,1,0:T(8,128)} %param.12) | copy-start | bytes 3145732
  27.0 10.6 %collective-permute-start.3 = (f32[512,128]{0,1:T(8,128)}, f32[512,128]{0,1:T(8,128)}, u32[]{:S(2)}, u32[]{:S(2)}) collective-permute-start(f32[512,128]{0,1:T(8,128)} %bitcast.19), channel_id=1, source_target_pairs={{0,4},{12,8},{16,20},{28,24},{32,36},{44,40},{48,52},{60,56},{64,6... | collective-permute-start | bytes 786440 | tf_op jit(solution)/shard_map/ppermute | solution.py:86
  41.5 0.7 copy-start.7
  42.2 78.4 %copy-start.3 = (f32[256,256]{1,0:T(8,128)S(1)}, f32[256,256]{1,0:T(8,128)}, u32[]{:S(2)}) copy-start(f32[256,256]{1,0:T(8,128)} %get-tuple-element.46) | copy-start | bytes 786436
  120.7 6.0 %copy-start.9 = (f32[2,128,128]{1,2,0:T(8,128)S(1)}, f32[2,128,128]{1,2,0:T(8,128)}, u32[]{:S(2)}) copy-start(f32[2,128,128]{1,2,0:T(8,128)} %custom-call.22) | copy-start | bytes 393220
  120.7 7.8 %copy-start.6 = (f32[1,1,256,256]{2,3,1,0:T(8,128)S(1)}, f32[1,1,256,256]{2,3,1,0:T(8,128)}, u32[]{:S(2)}) copy-start(f32[1,1,256,256]{2,3,1,0:T(8,128)} %copy.8) | copy-start | bytes 786436
  128.5 1.4 copy-start.4
  129.2 0.7 copy-start.2
  129.9 2.3 collective-permute-start.4
  132.2 0.7 copy-start.10
  133.9 62.9 %copy-start.5 = (f32[256,128]{0,1:T(8,128)S(1)}, f32[256,128]{0,1:T(8,128)}, u32[]{:S(2)}) copy-start(f32[256,128]{0,1:T(8,128)} %copy-done.4) | copy-start | bytes 393220
  134.1 0.7 copy-start.8
  201.4 57.0 %collective-permute-start.5 = (f32[256,256]{0,1:T(8,128)S(1)}, f32[256,256]{0,1:T(8,128)S(1)}, u32[]{:S(2)}, u32[]{:S(2)}) collective-permute-start(f32[256,256]{0,1:T(8,128)S(1)} %pad_maximum_fusion.3), channel_id=1, source_target_pairs={{4,0},{8,12},{20,16},{24,28},{36,32},{40,44},{52,48},{56,60},{68,6... | collective-permute-start | bytes 786440 | tf_op jit(solution)/shard_map/ppermute | solution.py:111
  202.7 2.0 collective-permute-start.6
  203.3 55.0 %collective-permute-start.7 = (f32[256,128]{0,1:T(8,128)S(1)}, f32[256,128]{0,1:T(8,128)S(1)}, u32[]{:S(2)}, u32[]{:S(2)}) collective-permute-start(f32[256,128]{0,1:T(8,128)S(1)} %add_add_fusion), channel_id=1, source_target_pairs={{4,12},{8,0},{20,28},{24,16},{36,44},{40,32},{52,60},{56,48},{68,7... | collective-permute-start | bytes 393224 | tf_op jit(solution)/shard_map/ppermute | solution.py:115

commit v2 on v1

--- a/solution.py
+++ b/solution.py
@@ -2,6 +2,7 @@
 import jax.numpy as jnp
 from jax import lax
 from jax.sharding import PartitionSpec as P
+from jax.experimental import pallas as pl
 
 WALL_RATIO = 8.0
 HIGHEST = lax.Precision.HIGHEST
@@ -42,9 +43,49 @@
     )
 
 
+def sweep_kernel(a_ref, o_ref):
+    n = a_ref.shape[0]
+    o_ref[...] = a_ref[...]
+    lane = lax.broadcasted_iota(jnp.int32, (1, n), 1)
+    sub = lax.broadcasted_iota(jnp.int32, (n, 1), 0)
+
+    def body(k, carry):
+        whole = o_ref[...]
+        row = o_ref[pl.ds(k, 1), :]
+        pick = lane == k
+        pivot = jnp.sum(jnp.where(pick, row, 0.0), axis=1, keepdims=True)
+        scale = 1.0 / pivot
+        lead = row * scale - jnp.where(pick, scale, 0.0)
+        column = jnp.sum(jnp.where(pick, whole, 0.0), axis=1, keepdims=True)
+        column = column - jnp.where(sub == k, 1.0, 0.0)
+        o_ref[...] = whole - column * lead
+        o_ref[pl.ds(k, 1), :] = lead - jnp.where(pick, 1.0, 0.0)
+        return carry
+
+    lax.fori_loop(0, n, body, 0)
+
+
+def neg_inverse(block):
+    n = block.shape[0]
+    return pl.pallas_call(
+        sweep_kernel,
+        out_shape=jax.ShapeDtypeStruct(block.shape, block.dtype),
+        cost_estimate=pl.CostEstimate(
+            flops=2 * n * n * n, bytes_accessed=8 * n * n, transcendentals=0
+        ),
+    )(block)
+
+
 def schur_solve(schur, stacked):
-    factor = jnp.linalg.cholesky(schur)
-    return jax.scipy.linalg.cho_solve((factor, True), stacked)
+    h = schur.shape[0] // 2
+    upper, right = schur[:h, :h], schur[:h, h:]
+    left, lower = schur[h:, :h], schur[h:, h:]
+    upper_inv = -neg_inverse(upper)
+    reach = dot(upper_inv, right)
+    lower_inv = -neg_inverse(lower - dot(left, reach))
+    first = dot(upper_inv, stacked[:h])
+    second = dot(lower_inv, stacked[h:] - dot(left, first))
+    return jnp.concatenate([first - dot(reach, second), second], axis=0)
 
 
 def dot(a, b):

time: 262 us -> 180 us (0.69)
  other arithmetic: 130 us -> 10.5 us
  Pallas kernels: 0 us -> 58.1 us
  local copies, waits for them, and re-layouts: 27 us -> 10.5 us
    another operation x18 -> x0, other arithmetic: 118 us -> none  [the longest x13 75.8 us: schur_solve(): factor = jnp.linalg.cholesky(schur)]
    pallas_call x0 -> x4, Pallas kernels: none -> 58.1 us  [neg_inverse(): pl.pallas_call(sweep_kernel, out_shape=jax.ShapeDtypeStruct(block.shape,...]
    another operation x16 -> x0, matrix products: 13.5 us -> none  [the longest x12 7.94 us: schur_solve(): return jax.scipy.linalg.cho_solve((factor, True), stacked)]
    another operation x18 -> x1, local copies, waits for them, and re-layouts: 13.1 us -> 1.01 us
    dot_general x5 -> x17, matrix products: 5.43 us -> 16.9 us  [dot(): return jnp.dot(a, b, precision=HIGHEST)]
    dynamic_slice x5 -> x2, local copies, waits for them, and re-layouts: 7.59 us -> 2.02 us  [take(): return lax.dynamic_slice_in_dim(block, start, size, axis=axis)]
    ppermute x1, starting transfers between devices: 4.66 us -> 8.75 us  [padded_2(): lax.ppermute(lax.slice_in_dim(block, 0, width, axis=dim), axis, backward)]
    ppermute x1, waiting for transfers between devices: 4.91 us -> 8.41 us  [on_device(): sent_data = lax.ppermute(neumann, 'box', inward)]
  transfers between devices with their start and end apart: 8 -> 8, of which waited for: 2 -> 2; matrix products, arithmetic and copies ran while one was open for 5% -> 7% of each run, Pallas kernels for 0% -> 0%
where the time goes in v2:
time: 180 us; the launch traced here: 178 us
  waiting for transfers between devices  60 us (33%)
  Pallas kernels  58.1 us (32%)
  starting transfers between devices  19.8 us (11%)
  matrix products  18.4 us (10%)
  local copies, waits for them, and re-layouts  10.5 us (6%)
  other arithmetic  10.5 us (6%)
    pallas_call x4, Pallas kernels, neg_inverse(): pl.pallas_call(sweep_kernel, out_shape=jax.ShapeDtypeStruct(block.shape,...  58.1 us
    ppermute x1, waiting for transfers between devices, on_device(): across = lax.ppermute(half, 'box', group_route(count, [(1, 3), (2, 0)]))  51.6 us
    dot_general x17, matrix products, dot(): return jnp.dot(a, b, precision=HIGHEST)  16.9 us
    ppermute x1, starting transfers between devices, padded_2(): lax.ppermute(lax.slice_in_dim(block, 0, width, axis=dim), axis, backward)  8.75 us
    ppermute x1, waiting for transfers between devices, on_device(): sent_data = lax.ppermute(neumann, 'box', inward)  8.41 us
    unnamed x25, local copies, waits for them, and re-layouts  3.76 us
  transfers between devices with their start and end apart: 8, of which 2 were waited for; matrix products, arithmetic and copies ran while one was open for 7% of the time, Pallas kernels for 0%

profile of v2, /device:TPU:1, one launch (start us, length us, event | category | flops | bytes accessed | tf_op | source)
XLA Modules:
  0.0 178.4 jit_solution(2673053010285319297)
XLA Ops:
  0.6 1.1 slice_bitcast_fusion.4
  1.7 1.8 %convert_element_type.11 = f32[1,3,8,16,16,128]{5,4,3,2,1,0:T(8,128)S(1)} convert(bf16[1,3,8,16,16,128]{5,4,3,2,1,0:T(8,128)(2,1)} %param.6) | non-fusion elementwise | flops 786432 | bytes 4718592 | tf_op jit(solution)/shard_map/convert_element_type | solution.py:26
  3.6 2.2 %subtract_multiply_fusion = (f32[8,16,16,128]{3,2,1,0:T(8,128)S(1)}, f32[8,16,16,128]{3,2,1,0:T(8,128)}, f32[8,16,16,128]{3,2,1,0:T(8,128)}) fusion(f32[1,3,8,16,16,128]{5,4,3,2,1,0:T(8,128)S(1)} %convert_element_type.11, f32[8,16,16]{2,1,0:T(8,128)S(1)} %get-tuple-element.14, f32[8,16,16]{2,1,0:T(8,128)S(1)} %get-tuple-element.12, ...), kind=kLoop, calls=%fused_computation.22 | loop fusion | flops 3145728 | bytes 6324224 | tf_op jit(solution)/shard_map/mul | solution.py:32
  5.9 8.7 %collective-permute-start.1 = (f32[8,16,1,128]{3,2,1,0:T(1,128)S(1)}, f32[8,16,1,128]{3,2,1,0:T(1,128)S(1)}, u32[]{:S(2)}, u32[]{:S(2)}) collective-permute-start(f32[8,16,1,128]{3,2,1,0:T(1,128)S(1)} %get-tuple-element.7), channel_id=1, source_target_pairs={{1,0},{2,1},{3,2},{5,4},{6,5},{7,6},{9,8},{10,9},{11,10},{13,12},{... | collective-permute-start | bytes 196616 | tf_op jit(solution)/shard_map/ppermute | solution.py:19
  14.7 1.9 %collective-permute-start.2 = (f32[8,16,1,128]{3,2,1,0:T(1,128)S(1)}, f32[8,16,1,128]{3,2,1,0:T(1,128)S(1)}, u32[]{:S(2)}, u32[]{:S(2)}) collective-permute-start(f32[8,16,1,128]{3,2,1,0:T(1,128)S(1)} %get-tuple-element.8), channel_id=1, source_target_pairs={{0,1},{1,2},{2,3},{4,5},{5,6},{6,7},{8,9},{9,10},{10,11},{12,13},{... | collective-permute-start | bytes 196616 | tf_op jit(solution)/shard_map/ppermute | solution.py:16
  16.6 1.9 %dynamic-slice_bitcast_fusion = f32[512,256]{1,0:T(8,128)} fusion(f32[1,1,512,512]{3,2,1,0:T(8,128)} %param.11, s32[]{:T(128)S(6)} %select_n.86), kind=kLoop, calls=%fused_computation.25 | loop fusion | bytes 1048580 | tf_op jit(solution)/shard_map/dynamic_slice | solution.py:103
  18.5 3.2 %collective-permute-start = (f32[512,256]{1,0:T(8,128)}, f32[512,256]{1,0:T(8,128)}, u32[]{:S(2)}, u32[]{:S(2)}) collective-permute-start(f32[512,256]{1,0:T(8,128)} %dynamic-slice_bitcast_fusion), channel_id=1, source_target_pairs={{0,4},{12,8},{16,20},{28,24},{32,36},{44,40},{48,52},{60,56},{64,6... | collective-permute-start | bytes 1572872 | tf_op jit(solution)/shard_map/ppermute | solution.py:116
  21.7 2.5 %fusion.6 = bf16[8,16,16,128]{3,2,1,0:T(8,128)(2,1)S(1)} fusion(f32[8,16,16,128]{3,2,1,0:T(8,128)} %get-tuple-element.5, f32[8,16,16,128]{3,2,1,0:T(8,128)} %get-tuple-element.6, f32[8,16,16,128]{3,2,1,0:T(8,128)S(1)} %get-tuple-element.4, f32[8,16,1,128]{3,2,1,0:T(1,128)S(1)} %collective-permute-done.2, f32[8,16,1,128]{3,2,1,0:T(1,128)S(1)} %collective-permute-done.1), kind=kLoop, calls=%fused_computation.14 | loop fusion | flops 2359296 | bytes 3801088 | tf_op jit(solution)/shard_map/convert_element_type | solution.py:123
  24.3 1.5 fusion
  25.8 2.0 %collective-permute-start.3 = (f32[512,128]{0,1:T(8,128)}, f32[512,128]{0,1:T(8,128)}, u32[]{:S(2)}, u32[]{:S(2)}) collective-permute-start(f32[512,128]{0,1:T(8,128)} %bitcast.15), channel_id=1, source_target_pairs={{0,4},{12,8},{16,20},{28,24},{32,36},{44,40},{48,52},{60,56},{64,6... | collective-permute-start | bytes 786440 | tf_op jit(solution)/shard_map/ppermute | solution.py:127
  28.0 1.0 constant_dynamic-slice_fusion
  29.8 8.4 %collective-permute-done.3 = f32[512,128]{0,1:T(8,128)} collective-permute-done((f32[512,128]{0,1:T(8,128)}, f32[512,128]{0,1:T(8,128)}, u32[]{:S(2)}, u32[]{:S(2)}) %collective-permute-start.3) | collective-permute-done | bytes 262176 | tf_op jit(solution)/shard_map/ppermute | solution.py:127
  38.2 1.6 bitcast_add_fusion.1
  40.8 1.1 bitcast_add_fusion
  43.3 14.5 %shard_map.77 = f32[128,128]{1,0:T(8,128)} custom-call(f32[128,128]{1,0:T(8,128)} %slice.142.a_ref), custom_call_target="tpu_custom_call" | custom-call | flops 4194304 | bytes 131072 | tf_op jit(solution)/shard_map/pallas_call | solution.py:70
  57.8 1.1 fusion.31
  58.9 1.2 fusion.18
  60.7 1.8 %fusion.41 = f32[128,384]{1,0:T(8,128)} fusion(f32[128,384]{1,0:T(8,128)S(1)} %fusion.18, f32[256,256]{1,0:T(8,128)} %copy-done.5), kind=kOutput, calls=%fused_computation.80 | convolution fusion | flops 75497472 | bytes 458752 | tf_op jit(solution)/shard_map/dot_general | solution.py:92
  62.6 1.7 slice_subtract_fusion.3.a_ref
  64.3 14.5 %shard_map.78 = f32[128,128]{1,0:T(8,128)} custom-call(f32[128,128]{1,0:T(8,128)} %slice_subtract_fusion.3.a_ref), custom_call_target="tpu_custom_call" | custom-call | flops 4194304 | bytes 131072 | tf_op jit(solution)/shard_map/pallas_call | solution.py:70
  78.8 1.4 fusion.21
  80.2 1.3 convolution_subtract_fusion.1
  83.1 1.3 convolution_negate_fusion
  85.2 14.5 %shard_map.79 = f32[128,128]{1,0:T(8,128)} custom-call(f32[128,128]{1,0:T(8,128)} %slice.156.a_ref), custom_call_target="tpu_custom_call" | custom-call | flops 4194304 | bytes 131072 | tf_op jit(solution)/shard_map/pallas_call | solution.py:70
  99.8 1.0 fusion.27
  101.8 1.0 fusion.29
  104.0 14.5 %shard_map.80 = f32[128,128]{1,0:T(8,128)} custom-call(f32[128,128]{1,0:T(8,128)} %slice_subtract_fusion.2.a_ref), custom_call_target="tpu_custom_call" | custom-call | flops 4194304 | bytes 131072 | tf_op jit(solution)/shard_map/pallas_call | solution.py:70
  118.5 1.0 fusion.26
  120.4 1.4 add_add_fusion
  121.8 1.3 collective-permute-start.5
  123.8 1.3 collective-permute-start.7
  125.1 51.6 %collective-permute-done.7 = f32[256,128]{0,1:T(8,128)S(1)} collective-permute-done((f32[256,128]{0,1:T(8,128)S(1)}, f32[256,128]{0,1:T(8,128)S(1)}, u32[]{:S(2)}, u32[]{:S(2)}) %collective-permute-start.7) | collective-permute-done | bytes 131104 | tf_op jit(solution)/shard_map/ppermute | solution.py:156
  (55 shorter events, 11.6 us)
Async XLA Ops:
  0.6 23.7 %copy-start = (bf16[1,1,512,2048]{3,2,1,0:T(8,128)(2,1)S(1)}, bf16[1,1,512,2048]{3,2,1,0:T(8,128)(2,1)}, u32[]{:S(2)}) copy-start(bf16[1,1,512,2048]{3,2,1,0:T(8,128)(2,1)} %param.10) | copy-start | bytes 6291460
  1.7 1.8 %copy-start.9 = (f32[1,8,16,16]{3,2,1,0:T(8,128)S(1)}, f32[1,8,16,16]{3,2,1,0:T(8,128)}, u32[]{:S(2)}) copy-start(f32[1,8,16,16]{3,2,1,0:T(8,128)} %param.8) | copy-start | bytes 24580
  1.7 1.8 %copy-start.10 = (s32[1,8,16,16]{3,2,1,0:T(8,128)S(1)}, s32[1,8,16,16]{3,2,1,0:T(8,128)}, u32[]{:S(2)}) copy-start(s32[1,8,16,16]{3,2,1,0:T(8,128)} %param.9) | copy-start | bytes 24580
  5.9 15.8 %collective-permute-start.1 = (f32[8,16,1,128]{3,2,1,0:T(1,128)S(1)}, f32[8,16,1,128]{3,2,1,0:T(1,128)S(1)}, u32[]{:S(2)}, u32[]{:S(2)}) collective-permute-start(f32[8,16,1,128]{3,2,1,0:T(1,128)S(1)} %get-tuple-element.7), channel_id=1, source_target_pairs={{1,0},{2,1},{3,2},{5,4},{6,5},{7,6},{9,8},{10,9},{11,10},{13,12},{... | collective-permute-start | bytes 196616 | tf_op jit(solution)/shard_map/ppermute | solution.py:19
  14.7 7.1 %collective-permute-start.2 = (f32[8,16,1,128]{3,2,1,0:T(1,128)S(1)}, f32[8,16,1,128]{3,2,1,0:T(1,128)S(1)}, u32[]{:S(2)}, u32[]{:S(2)}) collective-permute-start(f32[8,16,1,128]{3,2,1,0:T(1,128)S(1)} %get-tuple-element.8), channel_id=1, source_target_pairs={{0,1},{1,2},{2,3},{4,5},{5,6},{6,7},{8,9},{9,10},{10,11},{12,13},{... | collective-permute-start | bytes 196616 | tf_op jit(solution)/shard_map/ppermute | solution.py:16
  18.5 22.3 %collective-permute-start = (f32[512,256]{1,0:T(8,128)}, f32[512,256]{1,0:T(8,128)}, u32[]{:S(2)}, u32[]{:S(2)}) collective-permute-start(f32[512,256]{1,0:T(8,128)} %dynamic-slice_bitcast_fusion), channel_id=1, source_target_pairs={{0,4},{12,8},{16,20},{28,24},{32,36},{44,40},{48,52},{60,56},{64,6... | collective-permute-start | bytes 1572872 | tf_op jit(solution)/shard_map/ppermute | solution.py:116
  24.3 3.6 %copy-start.1 = (f32[1,1,512,512]{3,2,1,0:T(8,128)S(1)}, f32[1,1,512,512]{3,2,1,0:T(8,128)}, u32[]{:S(2)}) copy-start(f32[1,1,512,512]{3,2,1,0:T(8,128)} %param.11) | copy-start | bytes 3145732
  25.8 12.3 %collective-permute-start.3 = (f32[512,128]{0,1:T(8,128)}, f32[512,128]{0,1:T(8,128)}, u32[]{:S(2)}, u32[]{:S(2)}) collective-permute-start(f32[512,128]{0,1:T(8,128)} %bitcast.15), channel_id=1, source_target_pairs={{0,4},{12,8},{16,20},{28,24},{32,36},{44,40},{48,52},{60,56},{64,6... | collective-permute-start | bytes 786440 | tf_op jit(solution)/shard_map/ppermute | solution.py:127
  28.0 36.3 %copy-start.2 = (f32[256,256]{1,0:T(8,128)}, f32[256,256]{1,0:T(8,128)S(1)}, u32[]{:S(2)}) copy-start(f32[256,256]{1,0:T(8,128)S(1)} %dynamic-slice_bitcast_fusion.1) | copy-start | bytes 786436
  41.9 0.7 copy-start.5
  58.9 3.7 %copy-start.6 = (f32[128,128]{1,0:T(8,128)}, f32[128,128]{1,0:T(8,128)S(1)}, u32[]{:S(2)}) copy-start(f32[128,128]{1,0:T(8,128)S(1)} %fusion.31) | copy-start | bytes 196612
  60.1 0.7 copy-start.3
  78.8 3.1 %copy-start.7 = (f32[128,256]{0,1:T(8,128)S(1)}, f32[128,256]{0,1:T(8,128)}, u32[]{:S(2)}) copy-start(f32[128,256]{0,1:T(8,128)} %copy.24) | copy-start | bytes 393220
  82.4 2.1 %copy-start.4 = (f32[256,128]{1,0:T(8,128)}, f32[256,128]{1,0:T(8,128)S(1)}, u32[]{:S(2)}) copy-start(f32[256,128]{1,0:T(8,128)S(1)} %convolution_add_fusion) | copy-start | bytes 393220
  82.4 2.0 %collective-permute-start.4 = (f32[256,384]{1,0:T(8,128)S(1)}, f32[256,384]{1,0:T(8,128)S(1)}, u32[]{:S(2)}, u32[]{:S(2)}) collective-permute-start(f32[256,384]{1,0:T(8,128)S(1)} %pad_maximum_fusion.2), channel_id=1, source_target_pairs={{4,8},{8,4},{20,24},{24,20},{36,40},{40,36},{52,56},{56,52},{68,72... | collective-permute-start | bytes 1179656 | tf_op jit(solution)/shard_map/ppermute | solution.py:146
  84.5 0.8 copy-start.8
  121.8 54.9 %collective-permute-start.5 = (f32[256,256]{0,1:T(8,128)S(1)}, f32[256,256]{0,1:T(8,128)S(1)}, u32[]{:S(2)}, u32[]{:S(2)}) collective-permute-start(f32[256,256]{0,1:T(8,128)S(1)} %pad_maximum_fusion.3), channel_id=1, source_target_pairs={{4,0},{8,12},{20,16},{24,28},{36,32},{40,44},{52,48},{56,60},{68,6... | collective-permute-start | bytes 786440 | tf_op jit(solution)/shard_map/ppermute | solution.py:152
  123.1 2.0 %collective-permute-start.6 = (f32[256,128]{0,1:T(8,128)S(1)}, f32[256,128]{0,1:T(8,128)S(1)}, u32[]{:S(2)}, u32[]{:S(2)}) collective-permute-start(f32[256,128]{0,1:T(8,128)S(1)} %add_add_fusion), channel_id=1, source_target_pairs={{4,8},{8,4},{20,24},{24,20},{36,40},{40,36},{52,56},{56,52},{68,72... | collective-permute-start | bytes 393224 | tf_op jit(solution)/shard_map/ppermute | solution.py:155
  123.8 52.9 %collective-permute-start.7 = (f32[256,128]{0,1:T(8,128)S(1)}, f32[256,128]{0,1:T(8,128)S(1)}, u32[]{:S(2)}, u32[]{:S(2)}) collective-permute-start(f32[256,128]{0,1:T(8,128)S(1)} %add_add_fusion), channel_id=1, source_target_pairs={{4,12},{8,0},{20,28},{24,16},{36,44},{40,32},{52,60},{56,48},{68,7... | collective-permute-start | bytes 393224 | tf_op jit(solution)/shard_map/ppermute | solution.py:156

commit v3 on v2

--- a/solution.py
+++ b/solution.py
@@ -71,18 +71,23 @@
         sweep_kernel,
         out_shape=jax.ShapeDtypeStruct(block.shape, block.dtype),
         cost_estimate=pl.CostEstimate(
-            flops=2 * n * n * n, bytes_accessed=8 * n * n, transcendentals=0
+            flops=8000 * n * n * n, bytes_accessed=8 * n * n, transcendentals=0
         ),
     )(block)
 
 
-def schur_solve(schur, stacked):
+def inverse_parts(schur):
     h = schur.shape[0] // 2
-    upper, right = schur[:h, :h], schur[:h, h:]
-    left, lower = schur[h:, :h], schur[h:, h:]
-    upper_inv = -neg_inverse(upper)
-    reach = dot(upper_inv, right)
-    lower_inv = -neg_inverse(lower - dot(left, reach))
+    upper_inv = -neg_inverse(schur[:h, :h])
+    reach = dot(upper_inv, schur[:h, h:])
+    left = schur[h:, :h]
+    lower_inv = -neg_inverse(schur[h:, h:] - dot(left, reach))
+    return (upper_inv, reach, left, lower_inv)
+
+
+def apply_inverse(parts, stacked):
+    upper_inv, reach, left, lower_inv = parts
+    h = upper_inv.shape[0]
     first = dot(upper_inv, stacked[:h])
     second = dot(lower_inv, stacked[h:] - dot(left, first))
     return jnp.concatenate([first - dot(reach, second), second], axis=0)
@@ -103,7 +108,7 @@
     return lax.dynamic_slice_in_dim(block, start, size, axis=axis)
 
 
-def on_device(velocity, field, conductivity, wall_flags, leaf_solution, leaf_dtn):
+def upward(velocity, field, conductivity, wall_flags, leaf_solution, leaf_dtn):
     count = lax.axis_size("box")
     dtn_map = leaf_dtn[0, 0]
     width = dtn_map.shape[0] // 2
@@ -112,8 +117,13 @@
     near = (1 - odd) * width
     far = odd * width
 
+    own_nn = take(take(dtn_map, near, width, 0), near, width, 1)
+    own_nf = take(take(dtn_map, near, width, 0), far, width, 1)
+    own_fn = take(take(dtn_map, far, width, 0), near, width, 1)
+    own_ff = take(take(dtn_map, far, width, 0), far, width, 1)
+
     inward = group_route(count, [(0, 1), (3, 2)])
-    sent_map = lax.ppermute(take(dtn_map, near, width, 1), "box", inward)
+    part_nn = lax.ppermute(own_nn, "box", inward)
 
     flow_x, flow_y, flow_z = currents(velocity[0], field[0], conductivity[0], wall_flags[0])
     solution_map = leaf_solution[0, 0]
@@ -124,29 +134,28 @@
     neumann = jnp.dot(
         solution_map, source.reshape(cell_count, snaps), preferred_element_type=jnp.float32
     )
-    sent_data = lax.ppermute(neumann, "box", inward)
+    own_near = take(neumann, near, width, 0)
+    own_far = take(neumann, far, width, 0)
+    sent = lax.ppermute(jnp.concatenate([own_fn, own_near, own_far], axis=1), "box", inward)
 
-    own_nn = take(take(dtn_map, near, width, 0), near, width, 1)
-    own_nf = take(take(dtn_map, near, width, 0), far, width, 1)
-    own_fn = take(take(dtn_map, far, width, 0), near, width, 1)
-    own_ff = take(take(dtn_map, far, width, 0), far, width, 1)
-    part_nn = take(sent_map, far, width, 0)
-    part_fn = take(sent_map, near, width, 0)
-    schur = own_nn + part_nn
-    rhs = take(neumann, near, width, 0) + take(sent_data, far, width, 0)
-    solved = schur_solve(schur, jnp.concatenate([own_nf, rhs], axis=1))
-    solved_map = solved[:, :width]
-    first_face = -solved[:, width:]
+    parts = inverse_parts(own_nn + part_nn)
+    solved_map = apply_inverse(parts, own_nf)
     far_map = own_ff - dot(own_fn, solved_map)
-    cross_map = -dot(part_fn, solved_map)
-    far_data = take(neumann, far, width, 0) + dot(own_fn, first_face)
-    part_data = take(sent_data, near, width, 0) + dot(part_fn, first_face)
 
     swap = group_route(count, [(1, 2), (2, 1)])
-    other = lax.ppermute(jnp.concatenate([far_map, far_data], axis=1), "box", swap)
-    schur_two = far_map + other[:, :width]
-    rhs_two = far_data + other[:, width:]
-    interface_two = -schur_solve(schur_two, rhs_two)
+    other_map = lax.ppermute(far_map, "box", swap)
+    parts_two = inverse_parts(far_map + other_map)
+
+    part_fn = sent[:, :width]
+    snaps = neumann.shape[1]
+    part_near = sent[:, width : width + snaps]
+    part_far = sent[:, width + snaps :]
+    first_face = -apply_inverse(parts, own_near + part_near)
+    cross_map = -dot(part_fn, solved_map)
+    far_data = own_far + dot(own_fn, first_face)
+    part_data = part_far + dot(part_fn, first_face)
+    other_data = lax.ppermute(far_data, "box", swap)
+    interface_two = -apply_inverse(parts_two, far_data + other_data)
     half = part_data + dot(cross_map, interface_two)
 
     outer = lax.ppermute(
@@ -170,7 +179,7 @@
 
 def solution(mesh):
     return jax.shard_map(
-        on_device,
+        upward,
         mesh=mesh,
         in_specs=(
             P("box", None, None, None, "slab", None),

time: 180 us -> 147 us (0.82)
  waiting for transfers between devices: 60 us -> 25.1 us
  starting transfers between devices: 19.8 us -> 28 us
  local copies, waits for them, and re-layouts: 10.5 us -> 6.75 us
    ppermute x6 -> x7, waiting for transfers between devices: 60 us -> 22.1 us  [the longest x1 22.1 us: upward(): across = lax.ppermute(half, 'box', group_route(count, [(1, 3), (2, 0)]))]
    ppermute x6 -> x7, starting transfers between devices: 9.16 us -> 21.2 us  [the longest x1 9.1 us: upward(): lax.ppermute(jnp.concatenate([own_fn, own_near, own_far], axis=1), 'box',...]
    ppermute x1, starting transfers between devices: 8.75 us -> 1.92 us  [padded_2(): lax.ppermute(lax.slice_in_dim(block, 0, width, axis=dim), axis, backward)]
    ppermute x1, starting transfers between devices: 1.92 us -> 4.84 us  [padded_2(): lax.ppermute(lax.slice_in_dim(block, block.shape[dim] - width, None, axis...]
    ppermute x1, waiting for transfers between devices: 0.01 us -> 2.92 us  [padded_2(): lax.ppermute(lax.slice_in_dim(block, 0, width, axis=dim), axis, backward)]
    unnamed x25 -> x24, local copies, waits for them, and re-layouts: 3.76 us -> 2.25 us
    dot_general x17 -> x21, matrix products: 16.9 us -> 15.8 us  [dot(): return jnp.dot(a, b, precision=HIGHEST)]
  transfers between devices with their start and end apart: 8 -> 9, of which waited for: 2 -> 2; matrix products, arithmetic and copies ran while one was open for 7% -> 10% of each run, Pallas kernels for 0% -> 20%
where the time goes in v3:
time: 147 us; the launch traced here: 146 us
  Pallas kernels  58.1 us (40%)
  starting transfers between devices  28 us (19%)
  waiting for transfers between devices  25.1 us (17%)
  matrix products  16.7 us (11%)
  other arithmetic  10.4 us (7%)
  local copies, waits for them, and re-layouts  6.75 us (5%)
    pallas_call x4, Pallas kernels, neg_inverse(): pl.pallas_call(sweep_kernel, out_shape=jax.ShapeDtypeStruct(block.shape,...  58.1 us
    ppermute x1, waiting for transfers between devices, upward(): across = lax.ppermute(half, 'box', group_route(count, [(1, 3), (2, 0)]))  22.1 us
    dot_general x21, matrix products, dot(): return jnp.dot(a, b, precision=HIGHEST)  15.8 us
    ppermute x1, starting transfers between devices, upward(): lax.ppermute(jnp.concatenate([own_fn, own_near, own_far], axis=1), 'box',...  9.1 us
    ppermute x1, starting transfers between devices, upward(): part_nn = lax.ppermute(own_nn, 'box', inward)  7.55 us
    ppermute x1, starting transfers between devices, padded_2(): lax.ppermute(lax.slice_in_dim(block, block.shape[dim] - width, None, axis...  4.84 us
    convert_element_type x1, other arithmetic, upward(): source = divergence(flow_x, flow_y, padded).astype(jnp.bfloat16)  3.44 us
  transfers between devices with their start and end apart: 9, of which 2 were waited for; matrix products, arithmetic and copies ran while one was open for 10% of the time, Pallas kernels for 20%

profile of v3, /device:TPU:1, one launch (start us, length us, event | category | flops | bytes accessed | tf_op | source)
XLA Modules:
  0.0 146.2 jit_solution(18323054203099479168)
XLA Ops:
  0.7 2.1 %dynamic-slice_bitcast_fusion = (f32[256,256]{1,0:T(8,128)}, f32[1,1,256,256]{3,2,1,0:T(8,128)S(1)}) fusion(f32[1,1,512,512]{3,2,1,0:T(8,128)} %param.11, s32[]{:T(128)S(6)} %select_n.82, s32[]{:T(128)S(6)} %select_n.80), kind=kLoop, calls=%fused_computation.33 | loop fusion | bytes 1048584 | tf_op jit(solution)/shard_map/dynamic_slice | solution.py:108
  2.8 7.6 %collective-permute-start = (f32[256,256]{1,0:T(8,128)}, f32[256,256]{1,0:T(8,128)}, u32[]{:S(2)}, u32[]{:S(2)}) collective-permute-start(f32[256,256]{1,0:T(8,128)} %get-tuple-element.7), channel_id=1, source_target_pairs={{0,4},{12,8},{16,20},{28,24},{32,36},{44,40},{48,52},{60,56},{64,6... | collective-permute-start | bytes 786440 | tf_op jit(solution)/shard_map/ppermute | solution.py:126
  10.3 1.8 %convert_element_type.11 = f32[1,3,8,16,16,128]{5,4,3,2,1,0:T(8,128)S(1)} convert(bf16[1,3,8,16,16,128]{5,4,3,2,1,0:T(8,128)(2,1)} %param.6) | non-fusion elementwise | flops 786432 | bytes 4718592 | tf_op jit(solution)/shard_map/convert_element_type | solution.py:26
  12.2 2.2 %subtract_multiply_fusion = (f32[8,16,16,128]{3,2,1,0:T(8,128)S(1)}, f32[8,16,16,128]{3,2,1,0:T(8,128)}, f32[8,16,16,128]{3,2,1,0:T(8,128)}) fusion(f32[1,3,8,16,16,128]{5,4,3,2,1,0:T(8,128)S(1)} %convert_element_type.11, f32[8,16,16]{2,1,0:T(8,128)S(1)} %get-tuple-element.18, f32[8,16,16]{2,1,0:T(8,128)S(1)} %get-tuple-element.16, ...), kind=kLoop, calls=%fused_computation.24 | loop fusion | flops 3145728 | bytes 6324224 | tf_op jit(solution)/shard_map/mul | solution.py:32
  14.5 4.8 %collective-permute-start.3 = (f32[8,16,1,128]{3,2,1,0:T(1,128)S(1)}, f32[8,16,1,128]{3,2,1,0:T(1,128)}, u32[]{:S(2)}, u32[]{:S(2)}) collective-permute-start(f32[8,16,1,128]{3,2,1,0:T(1,128)S(1)} %get-tuple-element.10), channel_id=1, source_target_pairs={{0,1},{1,2},{2,3},{4,5},{5,6},{6,7},{8,9},{9,10},{10,11},{12,13},{... | collective-permute-start | bytes 196616 | tf_op jit(solution)/shard_map/ppermute | solution.py:16
  19.3 1.9 %collective-permute-start.2 = (f32[8,16,1,128]{3,2,1,0:T(1,128)S(1)}, f32[8,16,1,128]{3,2,1,0:T(1,128)}, u32[]{:S(2)}, u32[]{:S(2)}) collective-permute-start(f32[8,16,1,128]{3,2,1,0:T(1,128)S(1)} %get-tuple-element.9), channel_id=1, source_target_pairs={{1,0},{2,1},{3,2},{5,4},{6,5},{7,6},{9,8},{10,9},{11,10},{13,12},{... | collective-permute-start | bytes 196616 | tf_op jit(solution)/shard_map/ppermute | solution.py:19
  21.3 0.8 copy.8
  22.1 2.9 %collective-permute-done.2 = f32[8,16,1,128]{3,2,1,0:T(1,128)} collective-permute-done((f32[8,16,1,128]{3,2,1,0:T(1,128)S(1)}, f32[8,16,1,128]{3,2,1,0:T(1,128)}, u32[]{:S(2)}, u32[]{:S(2)}) %collective-permute-start.2) | collective-permute-done | bytes 65568 | tf_op jit(solution)/shard_map/ppermute | solution.py:19
  25.0 3.4 %fusion.6 = bf16[8,16,16,128]{3,2,1,0:T(8,128)(2,1)} fusion(f32[8,16,16,128]{3,2,1,0:T(8,128)} %get-tuple-element.5, f32[8,16,16,128]{3,2,1,0:T(8,128)} %get-tuple-element.6, f32[8,16,16,128]{3,2,1,0:T(8,128)S(1)} %get-tuple-element.4, f32[8,16,1,128]{3,2,1,0:T(1,128)} %collective-permute-done.3, f32[8,16,1,128]{3,2,1,0:T(1,128)} %collective-permute-done.2), kind=kLoop, calls=%fused_computation.16 | loop fusion | flops 2359296 | bytes 3801088 | tf_op jit(solution)/shard_map/convert_element_type | solution.py:133
  28.5 1.1 add.72
  30.2 14.5 %shard_map.77 = f32[128,128]{1,0:T(8,128)} custom-call(f32[128,128]{1,0:T(8,128)} %slice.154.a_ref), custom_call_target="tpu_custom_call" | custom-call | flops 16777216000 | bytes 131072 | tf_op jit(solution)/shard_map/pallas_call | solution.py:70
  44.7 1.3 fusion.16
  46.0 1.0 fusion.27
  47.1 0.8 slice_subtract_fusion.5.a_ref
  47.9 14.5 %shard_map.78 = f32[128,128]{1,0:T(8,128)} custom-call(f32[128,128]{1,0:T(8,128)} %slice_subtract_fusion.5.a_ref), custom_call_target="tpu_custom_call" | custom-call | flops 16777216000 | bytes 131072 | tf_op jit(solution)/shard_map/pallas_call | solution.py:70
  62.4 1.2 convolution_subtract_fusion.2
  63.7 1.1 fusion.39
  65.1 1.4 convolution_subtract_fusion
  67.2 0.8 fusion
  68.1 0.8 pad_maximum_fusion.2
  68.9 9.1 %collective-permute-start.4 = (f32[256,512]{0,1:T(8,128)}, f32[256,512]{0,1:T(8,128)}, u32[]{:S(2)}, u32[]{:S(2)}) collective-permute-start(f32[256,512]{0,1:T(8,128)} %pad_maximum_fusion.2), channel_id=1, source_target_pairs={{0,4},{12,8},{16,20},{28,24},{32,36},{44,40},{48,52},{60,56},{64,6... | collective-permute-start | bytes 1572872 | tf_op jit(solution)/shard_map/ppermute | solution.py:139
  78.7 14.5 %shard_map.79 = f32[128,128]{1,0:T(8,128)} custom-call(f32[128,128]{1,0:T(8,128)} %slice.158.a_ref), custom_call_target="tpu_custom_call" | custom-call | flops 16777216000 | bytes 131072 | tf_op jit(solution)/shard_map/pallas_call | solution.py:70
  93.2 1.0 fusion.20
  95.7 14.5 %shard_map.80 = f32[128,128]{1,0:T(8,128)} custom-call(f32[128,128]{1,0:T(8,128)} %slice_subtract_fusion.2.a_ref), custom_call_target="tpu_custom_call" | custom-call | flops 16777216000 | bytes 131072 | tf_op jit(solution)/shard_map/pallas_call | solution.py:70
  110.3 1.0 slice_add_fusion.1
  111.8 1.1 fusion.24
  114.2 1.5 %convolution_negate_fusion = f32[256,256]{1,0:T(8,128)S(1)} fusion(f32[256,512]{0,1:T(8,128)} %collective-permute-done.4, f32[128,256]{1,0:T(8,128)S(1)} %fusion.39, f32[128,256]{1,0:T(8,128)S(1)} %convolution_subtract_fusion.1), kind=kOutput, calls=%fused_computation.6 | convolution fusion | flops 201457664 | bytes 786432 | tf_op jit(solution)/shard_map/dot_general | solution.py:97
  117.6 1.4 fusion.15
  119.1 1.3 collective-permute-start.6
  121.0 1.3 collective-permute-start.8
  122.4 22.1 %collective-permute-done.8 = f32[256,128]{0,1:T(8,128)S(1)} collective-permute-done((f32[256,128]{0,1:T(8,128)S(1)}, f32[256,128]{0,1:T(8,128)S(1)}, u32[]{:S(2)}, u32[]{:S(2)}) %collective-permute-start.8) | collective-permute-done | bytes 131104 | tf_op jit(solution)/shard_map/ppermute | solution.py:165
  145.3 0.8 copy.16
  (59 shorter events, 9.0 us)
Async XLA Ops:
  0.6 66.6 %copy-start = (bf16[1,1,512,2048]{3,2,1,0:T(8,128)(2,1)S(1)}, bf16[1,1,512,2048]{3,2,1,0:T(8,128)(2,1)}, u32[]{:S(2)}) copy-start(bf16[1,1,512,2048]{3,2,1,0:T(8,128)(2,1)} %param.10) | copy-start | bytes 6291460
  2.8 9.3 %copy-start.7 = (f32[1,3,8,16,16]{4,3,2,1,0:T(8,128)S(1)}, f32[1,3,8,16,16]{4,3,2,1,0:T(8,128)}, u32[]{:S(2)}) copy-start(f32[1,3,8,16,16]{4,3,2,1,0:T(8,128)} %param.7) | copy-start | bytes 73732
  2.8 9.4 %copy-start.8 = (f32[1,8,16,16]{3,2,1,0:T(8,128)S(1)}, f32[1,8,16,16]{3,2,1,0:T(8,128)}, u32[]{:S(2)}) copy-start(f32[1,8,16,16]{3,2,1,0:T(8,128)} %param.8) | copy-start | bytes 24580
  2.8 9.4 %copy-start.9 = (s32[1,8,16,16]{3,2,1,0:T(8,128)S(1)}, s32[1,8,16,16]{3,2,1,0:T(8,128)}, u32[]{:S(2)}) copy-start(s32[1,8,16,16]{3,2,1,0:T(8,128)} %param.9) | copy-start | bytes 24580
  2.8 25.7 %collective-permute-start = (f32[256,256]{1,0:T(8,128)}, f32[256,256]{1,0:T(8,128)}, u32[]{:S(2)}, u32[]{:S(2)}) collective-permute-start(f32[256,256]{1,0:T(8,128)} %get-tuple-element.7), channel_id=1, source_target_pairs={{0,4},{12,8},{16,20},{28,24},{32,36},{44,40},{48,52},{60,56},{64,6... | collective-permute-start | bytes 786440 | tf_op jit(solution)/shard_map/ppermute | solution.py:126
  14.5 7.6 %collective-permute-start.3 = (f32[8,16,1,128]{3,2,1,0:T(1,128)S(1)}, f32[8,16,1,128]{3,2,1,0:T(1,128)}, u32[]{:S(2)}, u32[]{:S(2)}) collective-permute-start(f32[8,16,1,128]{3,2,1,0:T(1,128)S(1)} %get-tuple-element.10), channel_id=1, source_target_pairs={{0,1},{1,2},{2,3},{4,5},{5,6},{6,7},{8,9},{9,10},{10,11},{12,13},{... | collective-permute-start | bytes 196616 | tf_op jit(solution)/shard_map/ppermute | solution.py:16
  19.3 5.7 %collective-permute-start.2 = (f32[8,16,1,128]{3,2,1,0:T(1,128)S(1)}, f32[8,16,1,128]{3,2,1,0:T(1,128)}, u32[]{:S(2)}, u32[]{:S(2)}) collective-permute-start(f32[8,16,1,128]{3,2,1,0:T(1,128)S(1)} %get-tuple-element.9), channel_id=1, source_target_pairs={{1,0},{2,1},{3,2},{5,4},{6,5},{7,6},{9,8},{10,9},{11,10},{13,12},{... | collective-permute-start | bytes 196616 | tf_op jit(solution)/shard_map/ppermute | solution.py:19
  62.4 4.8 %copy-start.1 = (bf16[8,16,16,128]{3,2,1,0:T(8,128)(2,1)S(1)}, bf16[8,16,16,128]{3,2,1,0:T(8,128)(2,1)}, u32[]{:S(2)}) copy-start(bf16[8,16,16,128]{3,2,1,0:T(8,128)(2,1)} %fusion.6) | copy-start | bytes 1572868
  65.1 3.0 %copy-start.2 = (f32[1,1,256,256]{2,3,1,0:T(8,128)S(1)}, f32[1,1,256,256]{2,3,1,0:T(8,128)}, u32[]{:S(2)}) copy-start(f32[1,1,256,256]{2,3,1,0:T(8,128)} %copy.8) | copy-start | bytes 786436
  66.5 11.5 %collective-permute-start.1 = (f32[256,256]{1,0:T(8,128)S(1)}, f32[256,256]{1,0:T(8,128)S(1)}, u32[]{:S(2)}, u32[]{:S(2)}) collective-permute-start(f32[256,256]{1,0:T(8,128)S(1)} %convolution_subtract_fusion), channel_id=1, source_target_pairs={{4,8},{8,4},{20,24},{24,20},{36,40},{40,36},{52,56},{56,52},{68,72... | collective-permute-start | bytes 786440 | tf_op jit(solution)/shard_map/ppermute | solution.py:146
  68.9 41.4 %collective-permute-start.4 = (f32[256,512]{0,1:T(8,128)}, f32[256,512]{0,1:T(8,128)}, u32[]{:S(2)}, u32[]{:S(2)}) collective-permute-start(f32[256,512]{0,1:T(8,128)} %pad_maximum_fusion.2), channel_id=1, source_target_pairs={{0,4},{12,8},{16,20},{28,24},{32,36},{44,40},{48,52},{60,56},{64,6... | collective-permute-start | bytes 1572872 | tf_op jit(solution)/shard_map/ppermute | solution.py:139
  94.3 0.6 copy-start.4
  95.7 15.5 %copy-start.3 = (f32[128,128]{1,0:T(8,128)S(1)}, f32[128,128]{1,0:T(8,128)}, u32[]{:S(2)}) copy-start(f32[128,128]{1,0:T(8,128)} %shard_map.77) | copy-start | bytes 196612
  110.3 5.5 %copy-start.6 = (f32[128,128]{1,0:T(8,128)S(1)}, f32[128,128]{1,0:T(8,128)}, u32[]{:S(2)}) copy-start(f32[128,128]{1,0:T(8,128)} %shard_map.79) | copy-start | bytes 196612
  111.3 5.6 %copy-start.5 = (f32[128,128]{1,0:T(8,128)S(1)}, f32[128,128]{1,0:T(8,128)}, u32[]{:S(2)}) copy-start(f32[128,128]{1,0:T(8,128)} %copy-done.4) | copy-start | bytes 196612
  111.5 5.0 %copy-start.10 = (f32[128,128]{1,0:T(8,128)S(1)}, f32[128,128]{1,0:T(8,128)}, u32[]{:S(2)}) copy-start(f32[128,128]{1,0:T(8,128)} %shard_map.80) | copy-start | bytes 196612
  113.6 2.2 %collective-permute-start.5 = (f32[256,128]{0,1:T(8,128)S(1)}, f32[256,128]{0,1:T(8,128)S(1)}, u32[]{:S(2)}, u32[]{:S(2)}) collective-permute-start(f32[256,128]{0,1:T(8,128)S(1)} %convolution_add_fusion), channel_id=1, source_target_pairs={{4,8},{8,4},{20,24},{24,20},{36,40},{40,36},{52,56},{56,52},{68,72... | collective-permute-start | bytes 393224 | tf_op jit(solution)/shard_map/ppermute | solution.py:157
  119.1 25.4 %collective-permute-start.6 = (f32[256,256]{0,1:T(8,128)S(1)}, f32[256,256]{0,1:T(8,128)S(1)}, u32[]{:S(2)}, u32[]{:S(2)}) collective-permute-start(f32[256,256]{0,1:T(8,128)S(1)} %pad_maximum_fusion.4), channel_id=1, source_target_pairs={{4,0},{8,12},{20,16},{24,28},{36,32},{40,44},{52,48},{56,60},{68,6... | collective-permute-start | bytes 786440 | tf_op jit(solution)/shard_map/ppermute | solution.py:161
  120.4 2.0 %collective-permute-start.7 = (f32[256,128]{0,1:T(8,128)S(1)}, f32[256,128]{0,1:T(8,128)S(1)}, u32[]{:S(2)}, u32[]{:S(2)}) collective-permute-start(f32[256,128]{0,1:T(8,128)S(1)} %fusion.15), channel_id=1, source_target_pairs={{4,8},{8,4},{20,24},{24,20},{36,40},{40,36},{52,56},{56,52},{68,72... | collective-permute-start | bytes 393224 | tf_op jit(solution)/shard_map/ppermute | solution.py:164
  121.0 23.4 %collective-permute-start.8 = (f32[256,128]{0,1:T(8,128)S(1)}, f32[256,128]{0,1:T(8,128)S(1)}, u32[]{:S(2)}, u32[]{:S(2)}) collective-permute-start(f32[256,128]{0,1:T(8,128)S(1)} %fusion.15), channel_id=1, source_target_pairs={{4,12},{8,0},{20,28},{24,16},{36,44},{40,32},{52,60},{56,48},{68,7... | collective-permute-start | bytes 393224 | tf_op jit(solution)/shard_map/ppermute | solution.py:165
